TPU v7x, 32 devices: a whole 2x2x4 slice. The times are simulated.
32 devices in a mesh: dp: 4 (over z), pipe: 2 (over core), expert: 4 (over y, x).
Axes of the slice: x: 2, y: 2, z: 4, core: 2. Of those that a mesh axis runs over, the one named last changes fastest.
Arguments:
- tokens: bfloat16 [2, 96, 3072], P(None, 'expert'), may hold values from -6 to 6
- expert_ids: int32 [2, 2, 96, 2], P('pipe', None, 'expert'), may hold values from 0 to 3, all different within a row; in each aligned block of 24 rows (0 to 23, 24 to 47, ..., all dimensions but the last counted through in order) at most 16 rows name the same one
- gates: float32 [2, 2, 96, 2], P('pipe', None, 'expert'), may hold values from 0.1 to 1
- w_gate: bfloat16 [2, 4, 3072, 704], P('pipe', 'expert', None, 'dp'), may hold values from -0.109375 to 0.109375
- w_up: bfloat16 [2, 4, 3072, 704], P('pipe', 'expert', None, 'dp'), may hold values from -0.109375 to 0.109375
- w_down: bfloat16 [2, 4, 704, 3072], P('pipe', 'expert', 'dp'), may hold values from -0.3125 to 0.3125
Outputs:
- layer_out: bfloat16 [2, 2, 96, 3072], P('pipe', None, 'expert', 'dp')
Inputs may be any that keep to these rules, and one draw needn't show every extreme that they name: `expert_ids`: each token names 2 different experts in each layer. Among the tokens of one index of expert in one layer and micro-batch (aligned blocks of 24 tokens) no expert is named by more than 16 tokens, and in some block an expert is named by exactly 16.
All inputs are finite; a program needn't handle non-finite values.
Results may differ from a plain program's by a relative error of at most 0.0052.
Values may be sent and summed in bfloat16 or wider, within the bound.
No kernel may reach another device: no remote copies, remote signals or barrier semaphores. Data moves between devices by JAX's collectives and lax.ppermute only.
A program may use at most 64 MiB of HBM per device.

v0:
```python
import jax
import jax.numpy as jnp
from jax import lax
from jax.sharding import PartitionSpec as P

TOP = 2
CAP = 16


def passed_along(value, axis, by):
    length = lax.axis_size(axis)
    pairs = [(i, i + by) for i in range(length) if 0 <= i + by < length]
    return lax.ppermute(value, axis, pairs)


def build_maps(route_ids, route_gates, experts, rows_all):
    flat_ids = route_ids.reshape(-1)
    onehot = (flat_ids[:, None] == jnp.arange(experts, dtype=jnp.int32)[None, :]).astype(jnp.int32)
    before = jnp.cumsum(onehot, axis=0) - onehot
    placed = flat_ids * CAP + jnp.sum(before * onehot, axis=1)
    matches = jnp.arange(rows_all, dtype=jnp.int32)[:, None] == placed[None, :]
    dispatch_map = jnp.sum(matches.astype(jnp.float32).reshape(rows_all, -1, TOP), axis=2).astype(
        jnp.bfloat16
    )
    combine_map = jnp.sum(
        jnp.where(matches, route_gates.reshape(-1)[None, :], 0.0).reshape(rows_all, -1, TOP), axis=2
    )
    return (dispatch_map, combine_map)


def per_device(tokens, expert_ids, gates, w_gate, w_up, w_down):
    experts = lax.axis_size("expert")
    dp_size = lax.axis_size("dp")
    sections = lax.axis_size("pipe")
    micro_count = tokens.shape[0]
    tok_rows = tokens.shape[1]
    model_width = tokens.shape[2]
    unit_count = w_gate.shape[3]
    columns = model_width // dp_size
    rows_all = experts * CAP
    gate_local = w_gate[0, 0]
    up_local = w_up[0, 0]
    down_local = w_down[0, 0]
    section = lax.axis_index("pipe")
    is_first = section == 0
    column_start = lax.axis_index("dp") * columns
    outputs = jnp.zeros((1, micro_count, tok_rows, columns), jnp.bfloat16)
    carried = jnp.zeros((tok_rows, model_width), jnp.bfloat16)
    turns = micro_count + sections - 1
    for moment in range(turns):
        offset_micro = moment - section
        in_window = (offset_micro >= 0) & (offset_micro < micro_count)
        micro_index = jnp.clip(offset_micro, 0, micro_count - 1)
        own_rows = tokens[min(moment, micro_count - 1)]
        route_ids = lax.dynamic_index_in_dim(expert_ids[0], micro_index, 0, keepdims=False)
        route_gates = lax.dynamic_index_in_dim(gates[0], micro_index, 0, keepdims=False)
        dispatch_map, combine_map = build_maps(route_ids, route_gates, experts, rows_all)
        current = jnp.where(is_first, own_rows, carried)
        current_cols = lax.dynamic_slice_in_dim(current, column_start, columns, 1)
        outgoing = jnp.dot(dispatch_map, current, preferred_element_type=jnp.float32)
        outgoing = outgoing.astype(jnp.bfloat16).reshape(experts, CAP, model_width)
        arrived = lax.all_to_all(outgoing, "expert", split_axis=0, concat_axis=0, tiled=True)
        flat_rows = arrived.reshape(-1, model_width)
        squares = jnp.mean(jnp.square(flat_rows.astype(jnp.float32)), axis=1, keepdims=True)
        inv_rms = lax.rsqrt(squares + 1e-05)
        gate_act = jnp.dot(flat_rows, gate_local, preferred_element_type=jnp.float32) * inv_rms
        up_act = jnp.dot(flat_rows, up_local, preferred_element_type=jnp.float32) * inv_rms
        hidden_rows = (jax.nn.silu(gate_act) * up_act).astype(jnp.bfloat16)
        hidden = hidden_rows.reshape(arrived.shape[0], arrived.shape[1], unit_count)
        hidden = hidden.reshape(rows_all, unit_count)
        summed = lax.psum_scatter(
            lax.dot_general(
                down_local, hidden, (((0,), (1,)), ((), ())), preferred_element_type=jnp.float32
            ),
            "dp",
            scatter_dimension=0,
            tiled=True,
        )
        shares = summed.astype(jnp.bfloat16).reshape(columns, experts, CAP)
        returned = lax.all_to_all(
            shares, "expert", split_axis=1, concat_axis=1, tiled=True
        ).reshape(columns, rows_all)
        mixed = lax.dot_general(
            combine_map,
            returned.astype(jnp.float32),
            (((0,), (1,)), ((), ())),
            precision=lax.Precision.HIGHEST,
            preferred_element_type=jnp.float32,
        )
        new_cols = (current_cols.astype(jnp.float32) + mixed).astype(jnp.bfloat16)
        updated = lax.dynamic_update_slice_in_dim(outputs, new_cols[None, None], micro_index, 1)
        outputs = jnp.where(in_window, updated, outputs)
        if moment + 1 < turns:
            full_rows = lax.all_gather(new_cols, "dp", axis=1, tiled=True)
            carried = passed_along(full_rows, "pipe", 1)
    return outputs


def solution(mesh):
    return jax.shard_map(
        per_device,
        mesh=mesh,
        in_specs=(
            P(None, "expert", None),
            P("pipe", None, "expert", None),
            P("pipe", None, "expert", None),
            P("pipe", "expert", None, "dp"),
            P("pipe", "expert", None, "dp"),
            P("pipe", "expert", "dp", None),
        ),
        out_specs=P("pipe", None, "expert", "dp"),
        check_vma=False,
    )
```

profile of v0, /device:TPU:0, one launch (start us, length us, event | category | flops | bytes accessed | tf_op | source)
XLA Modules:
  0.0 198.9 jit_solution(14078611586446322383)
XLA Ops:
  10.1 12.1 %all_to_all.30 = bf16[4,16,3072]{2,1,0:T(8,128)(2,1)S(1)} all-to-all(bf16[4,16,3072]{2,1,0:T(8,128)(2,1)S(1)} %bitcast.104), channel_id=1, replica_groups=mesh['dp'=4,'pipe'=2,'expert'=4] {'expert'}, dimensions={0} | all-to-all | bytes 786432 | tf_op jit(solution)/shard_map/all_to_all | solution.py:62
  23.2 1.5 convolution_multiply_fusion.5
  24.8 2.8 %convolution_bitcast_fusion.2 = f32[3072,64]{0,1:T(8,128)} fusion(bf16[64,3072]{1,0:T(8,128)(2,1)} %bitcast.99, bf16[1,1,176,3072]{3,2,1,0:T(8,128)(2,1)S(1)} %copy-done, bf16[1,1,3072,176]{2,3,1,0:T(8,128)(2,1)S(1)} %copy-done.2, f32[64,176]{1,0:T(8,128)S(1)} %convolution_multiply_fusion.5, f32[64]{0:T(128)S(1)} %rsqrt.34), kind=kOutput, calls=%fused_computation.2 | convolution fusion | flops 138490880 | bytes 3387648 | tf_op jit(solution)/shard_map/dot_general | solution.py:72
  28.7 22.1 %reduce-scatter.4.cloned.1.call-done = f32[768,64]{0,1:T(8,128)} async-done(((f32[3072,64]{0,1:T(8,128)}), f32[768,64]{0,1:T(8,128)}) %reduce-scatter.4.cloned.1.call-update) | async-done | bytes 196624 | tf_op jit(solution)/shard_map/reduce_scatter | solution.py:71
  50.8 1.6 convert_element_type.101
  52.4 3.6 %all-to-all-start.1 = ((bf16[768,4,16]{0,2,1:T(8,128)(2,1)}), bf16[768,4,16]{0,2,1:T(8,128)(2,1)S(1)}, u32[]{:S(2)}, u32[]{:S(2)}) async-start(bf16[768,4,16]{0,2,1:T(8,128)(2,1)} %bitcast.110), calls=%async_computation.2 | async-start | bytes 196608 | tf_op jit(solution)/shard_map/all_to_all | solution.py:80
  56.4 4.6 %all-to-all-done.1 = bf16[768,4,16]{0,2,1:T(8,128)(2,1)S(1)} async-done(((bf16[768,4,16]{0,2,1:T(8,128)(2,1)}), bf16[768,4,16]{0,2,1:T(8,128)(2,1)S(1)}, u32[]{:S(2)}, u32[]{:S(2)}) %all-to-all-start.1) | async-done | bytes 98336 | tf_op jit(solution)/shard_map/all_to_all | solution.py:80
  61.2 13.5 %all_gather.6 = bf16[24,3072]{1,0:T(8,128)(2,1)S(1)} all-gather(bf16[24,768]{1,0:T(8,128)(2,1)S(1)} %get-tuple-element.20), channel_id=1, replica_groups=mesh['dp'=4,'pipe'=2,'expert'=4] {'dp'}, dimensions={1}, use_global_device_ids=true | all-gather | bytes 184320 | tf_op jit(solution)/shard_map/all_gather | solution.py:94
  78.1 10.3 %all_to_all.31 = bf16[4,16,3072]{2,1,0:T(8,128)(2,1)S(1)} all-to-all(bf16[4,16,3072]{2,1,0:T(8,128)(2,1)S(1)} %bitcast.105), channel_id=1, replica_groups=mesh['dp'=4,'pipe'=2,'expert'=4] {'expert'}, dimensions={0} | all-to-all | bytes 786432 | tf_op jit(solution)/shard_map/all_to_all | solution.py:62
  90.9 2.8 %convolution_bitcast_fusion.1 = f32[3072,64]{0,1:T(8,128)} fusion(bf16[64,3072]{1,0:T(8,128)(2,1)} %bitcast.101, bf16[1,1,176,3072]{3,2,1,0:T(8,128)(2,1)S(1)} %copy-done, bf16[1,1,3072,176]{2,3,1,0:T(8,128)(2,1)S(1)} %copy-done.2, f32[64,176]{1,0:T(8,128)S(1)} %convolution_multiply_fusion.3, f32[64]{0:T(128)S(1)} %rsqrt.36), kind=kOutput, calls=%fused_computation.1 | convolution fusion | flops 138490880 | bytes 3387648 | tf_op jit(solution)/shard_map/dot_general | solution.py:72
  93.8 21.2 %reduce-scatter.6.cloned.1.call-done = f32[768,64]{0,1:T(8,128)} async-done(((f32[3072,64]{0,1:T(8,128)}), f32[768,64]{0,1:T(8,128)}) %reduce-scatter.6.cloned.1.call-update) | async-done | bytes 196624 | tf_op jit(solution)/shard_map/reduce_scatter | solution.py:71
  115.1 1.6 convert_element_type.110
  116.6 3.7 %all-to-all-start.3 = ((bf16[768,4,16]{0,2,1:T(8,128)(2,1)}), bf16[768,4,16]{0,2,1:T(8,128)(2,1)S(1)}, u32[]{:S(2)}, u32[]{:S(2)}) async-start(bf16[768,4,16]{0,2,1:T(8,128)(2,1)} %bitcast.111), calls=%async_computation.5 | async-start | bytes 196608 | tf_op jit(solution)/shard_map/all_to_all | solution.py:80
  120.3 4.9 %all-to-all-done.3 = bf16[768,4,16]{0,2,1:T(8,128)(2,1)S(1)} async-done(((bf16[768,4,16]{0,2,1:T(8,128)(2,1)}), bf16[768,4,16]{0,2,1:T(8,128)(2,1)S(1)}, u32[]{:S(2)}, u32[]{:S(2)}) %all-to-all-start.3) | async-done | bytes 98336 | tf_op jit(solution)/shard_map/all_to_all | solution.py:80
  125.2 1.6 fusion.38
  126.8 13.4 %all_gather.7 = bf16[24,3072]{1,0:T(8,128)(2,1)S(1)} all-gather(bf16[24,768]{1,0:T(8,128)(2,1)S(1)} %get-tuple-element.12), channel_id=1, replica_groups=mesh['dp'=4,'pipe'=2,'expert'=4] {'dp'}, dimensions={1}, use_global_device_ids=true | all-gather | bytes 184320 | tf_op jit(solution)/shard_map/all_gather | solution.py:94
  143.7 10.3 %all_to_all.32 = bf16[4,16,3072]{2,1,0:T(8,128)(2,1)S(1)} all-to-all(bf16[4,16,3072]{2,1,0:T(8,128)(2,1)S(1)} %bitcast.106), channel_id=1, replica_groups=mesh['dp'=4,'pipe'=2,'expert'=4] {'expert'}, dimensions={0} | all-to-all | bytes 786432 | tf_op jit(solution)/shard_map/all_to_all | solution.py:62
  155.0 1.5 convolution_multiply_fusion.1
  156.5 2.9 %convolution_bitcast_fusion = f32[3072,64]{0,1:T(8,128)} fusion(bf16[64,3072]{1,0:T(8,128)(2,1)} %bitcast.103, bf16[1,1,176,3072]{3,2,1,0:T(8,128)(2,1)S(1)} %copy-done, bf16[1,1,3072,176]{2,3,1,0:T(8,128)(2,1)S(1)} %copy-done.2, f32[64,176]{1,0:T(8,128)S(1)} %convolution_multiply_fusion.1, f32[64]{0:T(128)S(1)} %rsqrt.38), kind=kOutput, calls=%fused_computation | convolution fusion | flops 138490880 | bytes 3387648 | tf_op jit(solution)/shard_map/dot_general | solution.py:72
  159.3 21.3 %reduce-scatter.8.cloned.1.call-done = f32[768,64]{0,1:T(8,128)} async-done(((f32[3072,64]{0,1:T(8,128)}), f32[768,64]{0,1:T(8,128)}) %reduce-scatter.8.cloned.1.call-update) | async-done | bytes 196624 | tf_op jit(solution)/shard_map/reduce_scatter | solution.py:71
  180.7 1.6 convert_element_type.119
  182.2 3.7 %all-to-all-start.5 = ((bf16[768,4,16]{0,2,1:T(8,128)(2,1)}), bf16[768,4,16]{0,2,1:T(8,128)(2,1)S(1)}, u32[]{:S(2)}, u32[]{:S(2)}) async-start(bf16[768,4,16]{0,2,1:T(8,128)(2,1)} %bitcast.27), calls=%async_computation.8 | async-start | bytes 196608 | tf_op jit(solution)/shard_map/all_to_all | solution.py:80
  185.9 4.9 %all-to-all-done.5 = bf16[768,4,16]{0,2,1:T(8,128)(2,1)S(1)} async-done(((bf16[768,4,16]{0,2,1:T(8,128)(2,1)}), bf16[768,4,16]{0,2,1:T(8,128)(2,1)S(1)}, u32[]{:S(2)}, u32[]{:S(2)}) %all-to-all-start.5) | async-done | bytes 98336 | tf_op jit(solution)/shard_map/all_to_all | solution.py:80
  190.8 1.6 fusion.37
  (70 shorter events, 16.6 us)
Async XLA Ops:
  6.5 18.2 %copy-start = (bf16[1,1,176,3072]{3,2,1,0:T(8,128)(2,1)S(1)}, bf16[1,1,176,3072]{3,2,1,0:T(8,128)(2,1)}, u32[]{:S(2)}) copy-start(bf16[1,1,176,3072]{3,2,1,0:T(8,128)(2,1)} %param.11) | copy-start | bytes 3244036
  6.5 44.3 %reduce-scatter.4.cloned.1.call-start = ((), (), s32[]{:S(2)}) async-start(), calls=%async_computation.9 | async-start | bytes 983040 | tf_op jit(solution)/shard_map/reduce_scatter | solution.py:71
  7.6 15.6 %copy-start.1 = (bf16[1,1,3072,176]{2,3,1,0:T(8,128)(2,1)S(1)}, bf16[1,1,3072,176]{2,3,1,0:T(8,128)(2,1)}, u32[]{:S(2)}) copy-start(bf16[1,1,3072,176]{2,3,1,0:T(8,128)(2,1)} %param.9) | copy-start | bytes 3244036
  22.2 0.7 copy-start.3
  23.0 1.8 copy-start.2
  52.4 8.6 %all-to-all-start.1 = ((bf16[768,4,16]{0,2,1:T(8,128)(2,1)}), bf16[768,4,16]{0,2,1:T(8,128)(2,1)S(1)}, u32[]{:S(2)}, u32[]{:S(2)}) async-start(bf16[768,4,16]{0,2,1:T(8,128)(2,1)} %bitcast.110), calls=%async_computation.2 | async-start | bytes 196608 | tf_op jit(solution)/shard_map/all_to_all | solution.py:80
  56.0 59.0 %reduce-scatter.6.cloned.1.call-start = ((), (), s32[]{:S(2)}) async-start(), calls=%async_computation.10 | async-start | bytes 983040 | tf_op jit(solution)/shard_map/reduce_scatter | solution.py:71
  61.2 16.7 %copy-start.6 = (bf16[1,2,24,768]{3,2,1,0:T(8,128)(2,1)}, bf16[1,2,24,768]{3,2,1,0:T(8,128)(2,1)S(1)}, u32[]{:S(2)}) copy-start(bf16[1,2,24,768]{3,2,1,0:T(8,128)(2,1)S(1)} %get-tuple-element.19) | copy-start | bytes 221188
  74.6 2.3 %collective-permute-start = (bf16[24,3072]{1,0:T(8,128)(2,1)S(1)}, bf16[24,3072]{1,0:T(8,128)(2,1)S(1)}, u32[]{:S(2)}, u32[]{:S(2)}) collective-permute-start(bf16[24,3072]{1,0:T(8,128)(2,1)S(1)} %all_gather.6), channel_id=1, source_target_pairs={{0,4},{1,5},{2,6},{3,7},{8,12},{9,13},{10,14},{11,15},{16,20},{17,... | collective-permute-start | bytes 442376 | tf_op jit(solution)/shard_map/ppermute | solution.py:13
  88.5 0.7 copy-start.4
  116.6 8.6 %all-to-all-start.3 = ((bf16[768,4,16]{0,2,1:T(8,128)(2,1)}), bf16[768,4,16]{0,2,1:T(8,128)(2,1)S(1)}, u32[]{:S(2)}, u32[]{:S(2)}) async-start(bf16[768,4,16]{0,2,1:T(8,128)(2,1)} %bitcast.111), calls=%async_computation.5 | async-start | bytes 196608 | tf_op jit(solution)/shard_map/all_to_all | solution.py:80
  120.3 60.4 %reduce-scatter.8.cloned.1.call-start = ((), (), s32[]{:S(2)}) async-start(), calls=%async_computation.11 | async-start | bytes 983040 | tf_op jit(solution)/shard_map/reduce_scatter | solution.py:71
  140.2 2.3 %collective-permute-start.1 = (bf16[24,3072]{1,0:T(8,128)(2,1)S(1)}, bf16[24,3072]{1,0:T(8,128)(2,1)S(1)}, u32[]{:S(2)}, u32[]{:S(2)}) collective-permute-start(bf16[24,3072]{1,0:T(8,128)(2,1)S(1)} %all_gather.7), channel_id=1, source_target_pairs={{0,4},{1,5},{2,6},{3,7},{8,12},{9,13},{10,14},{11,15},{16,20},{17,... | collective-permute-start | bytes 442376 | tf_op jit(solution)/shard_map/ppermute | solution.py:13
  154.0 0.7 copy-start.5
  182.2 8.6 %all-to-all-start.5 = ((bf16[768,4,16]{0,2,1:T(8,128)(2,1)}), bf16[768,4,16]{0,2,1:T(8,128)(2,1)S(1)}, u32[]{:S(2)}, u32[]{:S(2)}) async-start(bf16[768,4,16]{0,2,1:T(8,128)(2,1)} %bitcast.27), calls=%async_computation.8 | async-start | bytes 196608 | tf_op jit(solution)/shard_map/all_to_all | solution.py:80
Sparse Core Ops, SparseCore 0:
  27.8 23.0 reduce-scatter.3
  93.9 21.0 reduce-scatter.5
  159.5 21.1 reduce-scatter.7
where the time goes:
time: 200 us; the launch traced here: 199 us
  waiting for transfers between devices  81 us (40%)
  blocking collectives  59.6 us (30%)
  matrix products  17.2 us (9%)
  starting transfers between devices  13.5 us (7%)
  between operations  13.3 us (7%)
  other arithmetic  9.16 us (5%)
  local copies, waits for them, and re-layouts  5.17 us (3%)
    reduce_scatter x3, waiting for transfers between devices, per_device(): lax.psum_scatter(lax.dot_general(down_local, hidden, (((0,), (1,)), ((),...  64.7 us
    all_to_all x3, blocking collectives, per_device(): lax.all_to_all(outgoing, 'expert', split_axis=0, concat_axis=0, tiled=True)  32.7 us
    all_gather x2, blocking collectives, per_device(): full_rows = lax.all_gather(new_cols, 'dp', axis=1, tiled=True)  26.9 us
    all_to_all x3, waiting for transfers between devices, per_device(): lax.all_to_all(shares, 'expert', split_axis=1, concat_axis=1, tiled=True)  14.4 us
    all_to_all x3, starting transfers between devices, per_device(): lax.all_to_all(shares, 'expert', split_axis=1, concat_axis=1, tiled=True)  11 us
    dot_general x3, matrix products, per_device(): lax.dot_general(down_local, hidden, (((0,), (1,)), ((), ())), preferred_e...  8.54 us
    convert_element_type x3, other arithmetic, per_device(): shares = summed.astype(jnp.bfloat16).reshape(columns, experts, CAP)  4.68 us
    dot_general x3, matrix products, per_device(): jnp.dot(flat_rows, gate_local, preferred_element_type=jnp.float32) * inv_rms  4.54 us
  transfers between devices with their start and end apart: 8, of which 8 were waited for; matrix products, arithmetic and copies ran while one was open for 1% of the time, Pallas kernels for 0%

commit v1 on v0

--- a/solution.py
+++ b/solution.py
@@ -1,3 +1,4 @@
+import functools
 import jax
 import jax.numpy as jnp
 from jax import lax
@@ -5,6 +6,21 @@
 
 TOP = 2
 CAP = 16
+
+
+def ports_choose(unit, axis_tag):
+    return jnp.concatenate(
+        jax.lax.all_to_all(
+            jnp.stack(jnp.split(unit, jax.lax.axis_size(axis_tag), 1), 0),
+            axis_name=axis_tag,
+            split_axis=0,
+            concat_axis=0,
+        ),
+        1,
+    )
+
+
+_update_target = functools.partial(ports_choose, axis_tag="expert")
 
 
 def passed_along(value, axis, by):
@@ -77,9 +93,7 @@
             tiled=True,
         )
         shares = summed.astype(jnp.bfloat16).reshape(columns, experts, CAP)
-        returned = lax.all_to_all(
-            shares, "expert", split_axis=1, concat_axis=1, tiled=True
-        ).reshape(columns, rows_all)
+        returned = _update_target(shares).reshape(columns, rows_all)
         mixed = lax.dot_general(
             combine_map,
             returned.astype(jnp.float32),

time: 200 us -> 200 us (level)
  no operation moved by 1% of the time
where the time goes in v1:
time: 200 us; the launch traced here: 199 us
  waiting for transfers between devices  81 us (40%)
  blocking collectives  59.6 us (30%)
  matrix products  17.2 us (9%)
  starting transfers between devices  13.5 us (7%)
  between operations  13.3 us (7%)
  other arithmetic  9.21 us (5%)
  local copies, waits for them, and re-layouts  5.2 us (3%)
    reduce_scatter x3, waiting for transfers between devices, per_device(): lax.psum_scatter(lax.dot_general(down_local, hidden, (((0,), (1,)), ((),...  64.7 us
    all_to_all x3, blocking collectives, per_device(): lax.all_to_all(outgoing, 'expert', split_axis=0, concat_axis=0, tiled=True)  32.7 us
    all_gather x2, blocking collectives, per_device(): full_rows = lax.all_gather(new_cols, 'dp', axis=1, tiled=True)  26.9 us
    all_to_all x3, waiting for transfers between devices, ports_choose(): jax.lax.all_to_all(jnp.stack(jnp.split(unit, jax.lax.axis_size(axis_tag),...  14.4 us
    all_to_all x3, starting transfers between devices, ports_choose(): jax.lax.all_to_all(jnp.stack(jnp.split(unit, jax.lax.axis_size(axis_tag),...  10.9 us
    dot_general x3, matrix products, per_device(): lax.dot_general(down_local, hidden, (((0,), (1,)), ((), ())), preferred_e...  8.54 us
    dot_general x3, matrix products, per_device(): jnp.dot(flat_rows, gate_local, preferred_element_type=jnp.float32) * inv_rms  4.54 us
  transfers between devices with their start and end apart: 8, of which 8 were waited for; matrix products, arithmetic and copies ran while one was open for 1% of the time, Pallas kernels for 0%

profile of v1, /device:TPU:0, one launch (start us, length us, event | category | flops | bytes accessed | tf_op | source)
XLA Modules:
  0.0 199.0 jit_solution(8946367668423537628)
XLA Ops:
  10.1 12.1 %all_to_all.30 = bf16[4,16,3072]{2,1,0:T(8,128)(2,1)S(1)} all-to-all(bf16[4,16,3072]{2,1,0:T(8,128)(2,1)S(1)} %bitcast.134), channel_id=1, replica_groups=mesh['dp'=4,'pipe'=2,'expert'=4] {'expert'}, dimensions={0} | all-to-all | bytes 786432 | tf_op jit(solution)/shard_map/all_to_all | solution.py:78
  23.2 1.5 convolution_multiply_fusion.5
  24.8 2.8 %convolution_bitcast_fusion.2 = f32[3072,64]{0,1:T(8,128)} fusion(bf16[64,3072]{1,0:T(8,128)(2,1)} %bitcast.129, bf16[1,1,176,3072]{3,2,1,0:T(8,128)(2,1)S(1)} %copy-done, bf16[1,1,3072,176]{2,3,1,0:T(8,128)(2,1)S(1)} %copy-done.2, f32[64,176]{1,0:T(8,128)S(1)} %convolution_multiply_fusion.5, f32[64]{0:T(128)S(1)} %rsqrt.34), kind=kOutput, calls=%fused_computation.2 | convolution fusion | flops 138490880 | bytes 3387648 | tf_op jit(solution)/shard_map/dot_general | solution.py:88
  28.7 22.1 %reduce-scatter.4.cloned.1.call-done = f32[768,64]{0,1:T(8,128)} async-done(((f32[3072,64]{0,1:T(8,128)}), f32[768,64]{0,1:T(8,128)}) %reduce-scatter.4.cloned.1.call-update) | async-done | bytes 196624 | tf_op jit(solution)/shard_map/reduce_scatter | solution.py:87
  52.4 3.6 %all-to-all-start.1 = ((bf16[4,768,1,16]{1,3,2,0:T(8,128)(2,1)}), bf16[4,768,1,16]{1,3,2,0:T(8,128)(2,1)S(1)}, u32[]{:S(2)}, u32[]{:S(2)}) async-start(bf16[4,768,1,16]{1,3,2,0:T(8,128)(2,1)} %pad_maximum_fusion), calls=%async_computation.2 | async-start | bytes 196608 | tf_op jit(solution)/shard_map/all_to_all | solution.py:13
  56.4 4.6 %all-to-all-done.1 = bf16[4,768,1,16]{1,3,2,0:T(8,128)(2,1)S(1)} async-done(((bf16[4,768,1,16]{1,3,2,0:T(8,128)(2,1)}), bf16[4,768,1,16]{1,3,2,0:T(8,128)(2,1)S(1)}, u32[]{:S(2)}, u32[]{:S(2)}) %all-to-all-start.1) | async-done | bytes 98336 | tf_op jit(solution)/shard_map/all_to_all | solution.py:13
  61.2 13.5 %all_gather.6 = bf16[24,3072]{1,0:T(8,128)(2,1)S(1)} all-gather(bf16[24,768]{1,0:T(8,128)(2,1)S(1)} %get-tuple-element.32), channel_id=1, replica_groups=mesh['dp'=4,'pipe'=2,'expert'=4] {'dp'}, dimensions={1}, use_global_device_ids=true | all-gather | bytes 184320 | tf_op jit(solution)/shard_map/all_gather | solution.py:108
  74.7 1.3 collective-permute-start
  78.2 10.3 %all_to_all.31 = bf16[4,16,3072]{2,1,0:T(8,128)(2,1)S(1)} all-to-all(bf16[4,16,3072]{2,1,0:T(8,128)(2,1)S(1)} %bitcast.135), channel_id=1, replica_groups=mesh['dp'=4,'pipe'=2,'expert'=4] {'expert'}, dimensions={0} | all-to-all | bytes 786432 | tf_op jit(solution)/shard_map/all_to_all | solution.py:78
  89.5 1.5 convolution_multiply_fusion.3
  91.0 2.8 %convolution_bitcast_fusion.1 = f32[3072,64]{0,1:T(8,128)} fusion(bf16[64,3072]{1,0:T(8,128)(2,1)} %bitcast.131, bf16[1,1,176,3072]{3,2,1,0:T(8,128)(2,1)S(1)} %copy-done, bf16[1,1,3072,176]{2,3,1,0:T(8,128)(2,1)S(1)} %copy-done.2, f32[64,176]{1,0:T(8,128)S(1)} %convolution_multiply_fusion.3, f32[64]{0:T(128)S(1)} %rsqrt.36), kind=kOutput, calls=%fused_computation.1 | convolution fusion | flops 138490880 | bytes 3387648 | tf_op jit(solution)/shard_map/dot_general | solution.py:88
  93.9 21.2 %reduce-scatter.6.cloned.1.call-done = f32[768,64]{0,1:T(8,128)} async-done(((f32[3072,64]{0,1:T(8,128)}), f32[768,64]{0,1:T(8,128)}) %reduce-scatter.6.cloned.1.call-update) | async-done | bytes 196624 | tf_op jit(solution)/shard_map/reduce_scatter | solution.py:87
  116.7 3.7 %all-to-all-start.3 = ((bf16[4,768,1,16]{1,3,2,0:T(8,128)(2,1)}), bf16[4,768,1,16]{1,3,2,0:T(8,128)(2,1)S(1)}, u32[]{:S(2)}, u32[]{:S(2)}) async-start(bf16[4,768,1,16]{1,3,2,0:T(8,128)(2,1)} %pad_maximum_fusion.1), calls=%async_computation.5 | async-start | bytes 196608 | tf_op jit(solution)/shard_map/all_to_all | solution.py:13
  120.4 4.9 %all-to-all-done.3 = bf16[4,768,1,16]{1,3,2,0:T(8,128)(2,1)S(1)} async-done(((bf16[4,768,1,16]{1,3,2,0:T(8,128)(2,1)}), bf16[4,768,1,16]{1,3,2,0:T(8,128)(2,1)S(1)}, u32[]{:S(2)}, u32[]{:S(2)}) %all-to-all-start.3) | async-done | bytes 98336 | tf_op jit(solution)/shard_map/all_to_all | solution.py:13
  125.3 1.6 fusion.38
  126.8 13.4 %all_gather.7 = bf16[24,3072]{1,0:T(8,128)(2,1)S(1)} all-gather(bf16[24,768]{1,0:T(8,128)(2,1)S(1)} %get-tuple-element.12), channel_id=1, replica_groups=mesh['dp'=4,'pipe'=2,'expert'=4] {'dp'}, dimensions={1}, use_global_device_ids=true | all-gather | bytes 184320 | tf_op jit(solution)/shard_map/all_gather | solution.py:108
  140.2 1.3 collective-permute-start.1
  143.8 10.3 %all_to_all.32 = bf16[4,16,3072]{2,1,0:T(8,128)(2,1)S(1)} all-to-all(bf16[4,16,3072]{2,1,0:T(8,128)(2,1)S(1)} %bitcast.136), channel_id=1, replica_groups=mesh['dp'=4,'pipe'=2,'expert'=4] {'expert'}, dimensions={0} | all-to-all | bytes 786432 | tf_op jit(solution)/shard_map/all_to_all | solution.py:78
  155.1 1.5 convolution_multiply_fusion.1
  156.6 2.8 %convolution_bitcast_fusion = f32[3072,64]{0,1:T(8,128)} fusion(bf16[64,3072]{1,0:T(8,128)(2,1)} %bitcast.133, bf16[1,1,176,3072]{3,2,1,0:T(8,128)(2,1)S(1)} %copy-done, bf16[1,1,3072,176]{2,3,1,0:T(8,128)(2,1)S(1)} %copy-done.2, f32[64,176]{1,0:T(8,128)S(1)} %convolution_multiply_fusion.1, f32[64]{0:T(128)S(1)} %rsqrt.38), kind=kOutput, calls=%fused_computation | convolution fusion | flops 138490880 | bytes 3387648 | tf_op jit(solution)/shard_map/dot_general | solution.py:88
  159.4 21.3 %reduce-scatter.8.cloned.1.call-done = f32[768,64]{0,1:T(8,128)} async-done(((f32[3072,64]{0,1:T(8,128)}), f32[768,64]{0,1:T(8,128)}) %reduce-scatter.8.cloned.1.call-update) | async-done | bytes 196624 | tf_op jit(solution)/shard_map/reduce_scatter | solution.py:87
  182.4 3.6 %all-to-all-start.5 = ((bf16[4,768,1,16]{1,3,2,0:T(8,128)(2,1)}), bf16[4,768,1,16]{1,3,2,0:T(8,128)(2,1)S(1)}, u32[]{:S(2)}, u32[]{:S(2)}) async-start(bf16[4,768,1,16]{1,3,2,0:T(8,128)(2,1)} %pad_maximum_fusion.2), calls=%async_computation.8 | async-start | bytes 196608 | tf_op jit(solution)/shard_map/all_to_all | solution.py:13
  186.0 4.9 %all-to-all-done.5 = bf16[4,768,1,16]{1,3,2,0:T(8,128)(2,1)S(1)} async-done(((bf16[4,768,1,16]{1,3,2,0:T(8,128)(2,1)}), bf16[4,768,1,16]{1,3,2,0:T(8,128)(2,1)S(1)}, u32[]{:S(2)}, u32[]{:S(2)}) %all-to-all-start.5) | async-done | bytes 98336 | tf_op jit(solution)/shard_map/all_to_all | solution.py:13
  190.9 1.6 fusion.37
  (76 shorter events, 17.3 us)
Async XLA Ops:
  6.5 18.2 %copy-start = (bf16[1,1,176,3072]{3,2,1,0:T(8,128)(2,1)S(1)}, bf16[1,1,176,3072]{3,2,1,0:T(8,128)(2,1)}, u32[]{:S(2)}) copy-start(bf16[1,1,176,3072]{3,2,1,0:T(8,128)(2,1)} %param.11) | copy-start | bytes 3244036
  6.5 44.3 %reduce-scatter.4.cloned.1.call-start = ((), (), s32[]{:S(2)}) async-start(), calls=%async_computation.9 | async-start | bytes 983040 | tf_op jit(solution)/shard_map/reduce_scatter | solution.py:87
  7.6 15.6 %copy-start.1 = (bf16[1,1,3072,176]{2,3,1,0:T(8,128)(2,1)S(1)}, bf16[1,1,3072,176]{2,3,1,0:T(8,128)(2,1)}, u32[]{:S(2)}) copy-start(bf16[1,1,3072,176]{2,3,1,0:T(8,128)(2,1)} %param.9) | copy-start | bytes 3244036
  22.2 0.7 copy-start.3
  23.0 1.8 copy-start.2
  52.4 8.6 %all-to-all-start.1 = ((bf16[4,768,1,16]{1,3,2,0:T(8,128)(2,1)}), bf16[4,768,1,16]{1,3,2,0:T(8,128)(2,1)S(1)}, u32[]{:S(2)}, u32[]{:S(2)}) async-start(bf16[4,768,1,16]{1,3,2,0:T(8,128)(2,1)} %pad_maximum_fusion), calls=%async_computation.2 | async-start | bytes 196608 | tf_op jit(solution)/shard_map/all_to_all | solution.py:13
  56.1 59.0 %reduce-scatter.6.cloned.1.call-start = ((), (), s32[]{:S(2)}) async-start(), calls=%async_computation.10 | async-start | bytes 983040 | tf_op jit(solution)/shard_map/reduce_scatter | solution.py:87
  61.2 16.7 %copy-start.6 = (bf16[1,2,24,768]{3,2,1,0:T(8,128)(2,1)}, bf16[1,2,24,768]{3,2,1,0:T(8,128)(2,1)S(1)}, u32[]{:S(2)}) copy-start(bf16[1,2,24,768]{3,2,1,0:T(8,128)(2,1)S(1)} %get-tuple-element.31) | copy-start | bytes 221188
  74.7 2.3 %collective-permute-start = (bf16[24,3072]{1,0:T(8,128)(2,1)S(1)}, bf16[24,3072]{1,0:T(8,128)(2,1)S(1)}, u32[]{:S(2)}, u32[]{:S(2)}) collective-permute-start(bf16[24,3072]{1,0:T(8,128)(2,1)S(1)} %all_gather.6), channel_id=1, source_target_pairs={{0,4},{1,5},{2,6},{3,7},{8,12},{9,13},{10,14},{11,15},{16,20},{17,... | collective-permute-start | bytes 442376 | tf_op jit(solution)/shard_map/ppermute | solution.py:29
  88.5 0.7 copy-start.4
  116.7 8.6 %all-to-all-start.3 = ((bf16[4,768,1,16]{1,3,2,0:T(8,128)(2,1)}), bf16[4,768,1,16]{1,3,2,0:T(8,128)(2,1)S(1)}, u32[]{:S(2)}, u32[]{:S(2)}) async-start(bf16[4,768,1,16]{1,3,2,0:T(8,128)(2,1)} %pad_maximum_fusion.1), calls=%async_computation.5 | async-start | bytes 196608 | tf_op jit(solution)/shard_map/all_to_all | solution.py:13
  120.4 60.4 %reduce-scatter.8.cloned.1.call-start = ((), (), s32[]{:S(2)}) async-start(), calls=%async_computation.11 | async-start | bytes 983040 | tf_op jit(solution)/shard_map/reduce_scatter | solution.py:87
  140.2 2.3 %collective-permute-start.1 = (bf16[24,3072]{1,0:T(8,128)(2,1)S(1)}, bf16[24,3072]{1,0:T(8,128)(2,1)S(1)}, u32[]{:S(2)}, u32[]{:S(2)}) collective-permute-start(bf16[24,3072]{1,0:T(8,128)(2,1)S(1)} %all_gather.7), channel_id=1, source_target_pairs={{0,4},{1,5},{2,6},{3,7},{8,12},{9,13},{10,14},{11,15},{16,20},{17,... | collective-permute-start | bytes 442376 | tf_op jit(solution)/shard_map/ppermute | solution.py:29
  154.1 0.7 copy-start.5
  182.4 8.5 %all-to-all-start.5 = ((bf16[4,768,1,16]{1,3,2,0:T(8,128)(2,1)}), bf16[4,768,1,16]{1,3,2,0:T(8,128)(2,1)S(1)}, u32[]{:S(2)}, u32[]{:S(2)}) async-start(bf16[4,768,1,16]{1,3,2,0:T(8,128)(2,1)} %pad_maximum_fusion.2), calls=%async_computation.8 | async-start | bytes 196608 | tf_op jit(solution)/shard_map/all_to_all | solution.py:13
Sparse Core Ops, SparseCore 0:
  27.8 23.0 reduce-scatter.3
  94.0 21.0 reduce-scatter.5
  159.6 21.1 reduce-scatter.7
